TPU v7x, 128 devices: a whole 4x4x4 slice. The times are simulated.
128 devices in a mesh: batch: 8 (over y, core), seq: 16 (over x, z).
Axes of the slice: x: 4, y: 4, z: 4, core: 2. Of those that a mesh axis runs over, the one named last changes fastest.
Arguments:
- frames: bfloat16 [8, 3072, 1024], P('batch', 'seq'), may hold values from -6 to 6
- lengths: int32 [8], P('batch'), may hold values from 768 to 3072, as said below
- w_qkv: bfloat16 [1024, 3072], replicated, may hold values from -0.25 to 0.25
- w_out: bfloat16 [1024, 1024], replicated, may hold values from -0.1875 to 0.1875
- cotangent: bfloat16 [8, 3072, 1024], P('batch', 'seq'), may hold values from -6 to 6
Outputs:
- output: bfloat16 [8, 3072, 1024], P('batch', 'seq')
- grad_input: bfloat16 [8, 3072, 1024], P('batch', 'seq')
- grad_qkv: float32 [1024, 3072], P('seq')
- grad_out: float32 [1024, 1024], P('seq')
Inputs may be any that keep to these rules, and one draw needn't show every extreme that they name: `lengths`: at least one utterance has all 3072 frames valid.
All inputs are finite; a program needn't handle non-finite values.
Results may differ from a plain program's by a relative error of at most 0.012.
The roundings to bfloat16 on the way count: a program that leaves them out, or rounds other values in their place, can miss the bound.
Values may be sent and summed in bfloat16 or wider, within the bound.
No kernel may reach another device: no remote copies, remote signals or barrier semaphores. Data moves between devices by JAX's collectives and lax.ppermute only.
A program may use at most 128 MiB of HBM per device.

v0:
```python
import jax
import jax.numpy as jnp
from jax import lax
from jax.sharding import PartitionSpec as P

H = 8


def from_partner(array, axis, stride):
    return lax.ppermute(array, axis, [(i, i ^ 1 << stride) for i in range(lax.axis_size(axis))])


def layer_norm(values):
    mean = jnp.mean(values, axis=-1, keepdims=True)
    centred = values - mean
    var = jnp.mean(centred * centred, axis=-1, keepdims=True)
    return centred * lax.rsqrt(var + 1e-05)


def block_forward(query_rows, keys, values, bias, scale):
    scores = jnp.dot(query_rows, keys.T, preferred_element_type=jnp.float32) * scale + bias[None, :]
    top = jnp.max(scores, axis=1, keepdims=True)
    expo = jnp.exp(scores - top)
    probs = expo / jnp.sum(expo, axis=1, keepdims=True)
    p_half = probs.astype(jnp.bfloat16)
    return (probs, p_half, jnp.dot(p_half, values, preferred_element_type=jnp.float32))


def head_backward(query, keys, values, dcontext, bias, scale):
    total, width = query.shape
    rows = min(512, total)
    qblocks = query.reshape(total // rows, rows, width)
    dblocks = dcontext.reshape(total // rows, rows, width)
    key_count = keys.shape[0]

    def step(carry, item):
        dkeys, dvalues = carry
        query_rows, d_rows = item
        probs, p_half, unused = block_forward(query_rows, keys, values, bias, scale)
        dprobs = jnp.dot(d_rows, values.T, preferred_element_type=jnp.float32)
        delta = jnp.sum(probs * dprobs, axis=1, keepdims=True)
        dscores = (probs * (dprobs - delta)).astype(jnp.bfloat16)
        dquery = jnp.dot(dscores, keys, preferred_element_type=jnp.float32) * scale
        dkeys = dkeys + jnp.dot(dscores.T, query_rows, preferred_element_type=jnp.float32) * scale
        dvalues = dvalues + jnp.dot(p_half.T, d_rows, preferred_element_type=jnp.float32)
        return ((dkeys, dvalues), dquery.astype(jnp.bfloat16))

    start = (jnp.zeros((key_count, width), jnp.float32), jnp.zeros((key_count, width), jnp.float32))
    (dkeys, dvalues), dquery = lax.scan(step, start, (qblocks, dblocks))
    return (dquery.reshape(total, width), dkeys, dvalues)


def to_heads(rows_array, groups, head_blocks):
    tok_rows, heads, head_size = rows_array.shape
    local_heads = heads // head_blocks
    part_rows = tok_rows // groups
    shaped = rows_array.reshape(groups, part_rows, head_blocks, local_heads, head_size)
    return shaped.transpose(2, 0, 1, 3, 4).reshape(
        head_blocks * groups, part_rows, local_heads, head_size
    )


def per_device(frames, lengths, w_qkv, w_out, cotangent):
    width = w_out.shape[0]
    head_size = width // H
    scale = float(head_size) ** (-0.5)
    tok_rows = frames.shape[1]
    seq_count = lax.axis_size("seq")
    groups = max(1, seq_count // H)
    local_heads = max(1, H // seq_count)
    head_blocks = H // local_heads
    part_rows = tok_rows // groups
    frame_total = tok_rows * seq_count
    group_index = lax.axis_index("seq") % groups
    length = lengths[0]
    inputs = frames[0].astype(jnp.float32)
    normed = layer_norm(inputs).astype(jnp.bfloat16)
    qkv = jnp.dot(normed, w_qkv, preferred_element_type=jnp.float32).astype(jnp.bfloat16)
    qkv_local = qkv.reshape(tok_rows, 3, H, head_size)
    query_send = to_heads(qkv_local[:, 0], groups, head_blocks)
    paired = (
        qkv_local[:, 1:]
        .reshape(tok_rows, 2, head_blocks, local_heads, head_size)
        .transpose(2, 0, 1, 3, 4)
    )
    paired_send = jnp.broadcast_to(
        paired[:, None], (head_blocks, groups, tok_rows, 2, local_heads, head_size)
    )
    paired_send = paired_send.reshape(seq_count, tok_rows, 2, local_heads, head_size)
    query_recv, paired_recv = (
        lax.all_to_all(query_send, "seq", split_axis=0, concat_axis=0, tiled=True),
        lax.all_to_all(paired_send, "seq", split_axis=0, concat_axis=0, tiled=True),
    )
    queries = query_recv.reshape(seq_count * part_rows, local_heads, head_size)
    keys = paired_recv[:, :, 0].reshape(frame_total, local_heads, head_size)
    values = paired_recv[:, :, 1].reshape(frame_total, local_heads, head_size)
    position = jnp.arange(frame_total, dtype=jnp.int32)
    bias = jnp.where(position < length, 0.0, -1000000000.0).astype(jnp.float32)
    offset = lax.axis_index("seq") * tok_rows
    own_pos = offset + jnp.arange(tok_rows, dtype=jnp.int32)
    valid = (own_pos < length).astype(jnp.float32)
    query = qkv_local[:, 0]
    top = jnp.full((H, tok_rows), -1e30, jnp.float32)
    key_piece = lax.all_gather(qkv_local[:, 1], "seq", axis=0, tiled=True)
    value_piece = lax.all_gather(qkv_local[:, 2], "seq", axis=0, tiled=True)
    key_pos = jnp.arange(key_piece.shape[0], dtype=jnp.int32)
    key_bias = jnp.where(key_pos < length, 0.0, -1000000000.0).astype(jnp.float32)
    scores = (
        jnp.einsum("qhd,khd->hqk", query, key_piece, preferred_element_type=jnp.float32) * scale
    )
    scores = scores + key_bias[None, None, :]
    new_top = jnp.maximum(top, jnp.max(scores, axis=2))
    expo = jnp.exp(scores - new_top[:, :, None])
    total = jnp.sum(expo, axis=2)
    accum = jnp.einsum(
        "hqk,khd->hqd", expo.astype(jnp.bfloat16), value_piece, preferred_element_type=jnp.float32
    )
    top, total, accum = (new_top, total, accum)
    context = (
        (accum / total[:, :, None]).astype(jnp.bfloat16).transpose(1, 0, 2).reshape(tok_rows, width)
    )
    branch = jnp.dot(context, w_out, preferred_element_type=jnp.float32)
    output = (inputs + valid[:, None] * branch).astype(jnp.bfloat16)
    grad_rows = (cotangent[0].astype(jnp.float32) * valid[:, None]).astype(jnp.bfloat16)
    columns = context
    out_share = lax.psum_scatter(
        jnp.dot(columns.T, grad_rows, preferred_element_type=jnp.float32),
        "seq",
        scatter_dimension=0,
        tiled=True,
    )
    dcontext = jnp.dot(grad_rows, w_out.T, preferred_element_type=jnp.float32).astype(jnp.bfloat16)
    dcontext_send = to_heads(dcontext.reshape(tok_rows, H, head_size), groups, head_blocks)
    dcontext_heads = lax.all_to_all(dcontext_send, "seq", split_axis=0, concat_axis=0, tiled=True)
    dcontext_heads = dcontext_heads.reshape(seq_count * part_rows, local_heads, head_size)
    dquery, dkeys, dvalues = head_backward(
        queries[:, 0], keys[:, 0], values[:, 0], dcontext_heads[:, 0], bias, scale
    )
    query_grads = [dquery]
    paired_grads = [jnp.stack([dkeys, dvalues], axis=1)]
    query_block = jnp.stack(query_grads, axis=1).reshape(
        seq_count, part_rows, 1, local_heads, head_size
    )
    paired_block = jnp.stack(paired_grads, axis=2)
    split_grads = paired_block.reshape(seq_count, groups, part_rows, 2, local_heads, head_size)
    own_half = lax.dynamic_index_in_dim(split_grads, group_index, 1, keepdims=False)
    other_half = lax.dynamic_index_in_dim(split_grads, 1 - group_index, 1, keepdims=False)
    partner_half = from_partner(other_half, "seq", 0)
    paired_rows = (own_half + partner_half).astype(jnp.bfloat16)
    dtrio = jnp.concatenate([query_block, paired_rows], axis=2)
    returned_grads = lax.all_to_all(dtrio, "seq", split_axis=0, concat_axis=0, tiled=True)
    dqkv = returned_grads.reshape(head_blocks, groups, part_rows, 3, local_heads, head_size)
    dqkv = dqkv.transpose(1, 2, 3, 0, 4, 5).reshape(tok_rows, 3 * width)
    columns = normed
    qkv_share = lax.psum_scatter(
        jnp.dot(columns.T, dqkv, preferred_element_type=jnp.float32),
        "seq",
        scatter_dimension=0,
        tiled=True,
    )
    grad_qkv, grad_out = lax.psum((qkv_share, out_share), "batch")
    dnormed = jnp.dot(dqkv, w_qkv.T, preferred_element_type=jnp.float32)
    unused, pull = jax.vjp(layer_norm, inputs)
    grad_input = (cotangent[0].astype(jnp.float32) + pull(dnormed)[0]).astype(jnp.bfloat16)
    return (output[None], grad_input[None], grad_qkv, grad_out)


def solution(mesh):
    return jax.shard_map(
        per_device,
        mesh=mesh,
        in_specs=(P("batch", "seq", None), P("batch"), P(), P(), P("batch", "seq", None)),
        out_specs=(
            P("batch", "seq", None),
            P("batch", "seq", None),
            P("seq", None),
            P("seq", None),
        ),
        check_vma=False,
    )
```

profile of v0, /device:TPU:0, one launch (start us, length us, event | category | flops | bytes accessed | tf_op | source)
XLA Modules:
  0.0 485.5 jit_solution(13089522208990970412)
XLA Ops:
  7.2 1.3 convert_reduce_fusion
  8.5 1.2 fusion.73
  10.3 4.4 fusion.38
  15.0 1.1 fusion.104
  16.1 0.8 copy.42
  16.9 1.8 copy.43
  19.1 1.5 broadcast_in_dim.61
  20.6 8.0 %all-to-all-start.1 = ((bf16[16,192,2,1,128]{4,1,3,2,0:T(8,128)(2,1)}), bf16[16,192,2,1,128]{4,1,3,2,0:T(8,128)(2,1)}, u32[]{:S(2)}, u32[]{:S(2)}) async-start(bf16[16,192,2,1,128]{4,1,3,2,0:T(8,128)(2,1)} %bitcast.192), calls=%async_computation.1 | async-start | bytes 3145728 | tf_op jit(solution)/shard_map/all_to_all | solution.py:92
  28.7 0.8 copy.41
  30.3 0.9 fusion.47
  31.2 0.8 copy.35
  32.0 26.6 %all-to-all-done.1 = bf16[16,192,2,1,128]{4,1,3,2,0:T(8,128)(2,1)} async-done(((bf16[16,192,2,1,128]{4,1,3,2,0:T(8,128)(2,1)}), bf16[16,192,2,1,128]{4,1,3,2,0:T(8,128)(2,1)}, u32[]{:S(2)}, u32[]{:S(2)}) %all-to-all-start.1) | async-done | bytes 1572896 | tf_op jit(solution)/shard_map/all_to_all | solution.py:92
  58.7 3.6 all-to-all-start
  62.2 2.4 fusion.103
  64.6 31.5 %all-gather.5.cloned.1.call-done = bf16[3072,1,8,128]{3,0,2,1:T(8,128)(2,1)} async-done(((bf16[192,1,8,128]{3,0,2,1:T(8,128)(2,1)}), bf16[3072,1,8,128]{3,0,2,1:T(8,128)(2,1)}) %all-gather.5.cloned.1.call-update) | async-done | bytes 6291472 | tf_op jit(solution)/shard_map/all_gather | solution.py:104
  96.1 12.2 %fusion.26 = (f32[8,192]{1,0:T(8,128)S(1)}, f32[8,192,3072]{2,1,0:T(8,128)}) fusion(f32[3072]{0:T(1024)S(1)} %fusion.98, bf16[3072,1,8,128]{3,0,2,1:T(8,128)(2,1)} %all-gather.5.cloned.1.call-done, bf16[192,1,8,128]{3,2,1,0:T(8,128)(2,1)} %get-tuple-element.117), kind=kOutput, calls=%fused_computation.34 | convolution fusion | flops 1222113792 | bytes 25577472 | tf_op jit(solution)/shard_map/qhd,khd->hqk/dot_general | solution.py:109
  108.3 10.3 %fusion.27 = f32[8,192]{1,0:T(8,128)S(1)} fusion(f32[8,192,3072]{2,1,0:T(8,128)} %get-tuple-element.121, f32[8,192]{1,0:T(8,128)S(1)} %broadcast_maximum_fusion, f32[3072]{0:T(1024)S(1)} %fusion.98), kind=kLoop, calls=%fused_computation.35 | loop fusion | flops 18872832 | bytes 18898944 | tf_op jit(solution)/shard_map/reduce_sum | solution.py:114
  118.6 4.5 all-to-all-start.2
  123.4 35.3 %all-gather.7.cloned.1.call-done = bf16[3072,1,8,128]{3,0,2,1:T(8,128)(2,1)} async-done(((bf16[192,1,8,128]{3,0,2,1:T(8,128)(2,1)}), bf16[3072,1,8,128]{3,0,2,1:T(8,128)(2,1)}) %all-gather.7.cloned.1.call-update) | async-done | bytes 6291472 | tf_op jit(solution)/shard_map/all_gather | solution.py:105
  158.7 10.5 %fusion.65 = bf16[8,24,8,128]{3,2,1,0:T(8,128)(2,1)S(1)} fusion(bf16[3072,1,8,128]{3,0,2,1:T(8,128)(2,1)} %all-gather.7.cloned.1.call-done, f32[8,192,3072]{2,1,0:T(8,128)} %get-tuple-element.121, f32[8,192]{1,0:T(8,128)S(1)} %broadcast_maximum_fusion, f32[3072]{0:T(1024)S(1)} %fusion.98, f32[192,8]{0,1:T(8,128)S(1)} %bitcast.199), kind=kOutput, calls=%fused_computation.76 | convolution fusion | flops 1227227136 | bytes 25583616 | tf_op jit(solution)/shard_map/hqk,khd->hqd/dot_general | solution.py:115
  169.2 0.7 copy-done.10
  169.9 2.7 fusion.83
  172.8 68.9 %while.15 = (s32[]{:T(128)}, f32[3072,128]{1,0:T(8,128)}, f32[3072,128]{1,0:T(8,128)}, bf16[3,512,128]{2,1,0:T(8,128)(2,1)}, bf16[3,512,128]{2,1,0:T(8,128)(2,1)...) while((s32[]{:T(128)}, f32[3072,128]{1,0:T(8,128)}, ...), condition=%wide.region_8.9_spmd.clone, body=%wide.region_4.0_spmd.clone.sunk | while | flops 2054689280 | bytes 116358872 | solution.py:49
  173.4 1.1 fusion.138
  174.5 2.7 copy-done.1
  177.2 1.4 fusion.139
  178.6 5.8 %convolution_add_fusion.2 = f32[3072,128]{1,0:T(8,128)} fusion(f32[3072,128]{1,0:T(8,128)} %get-tuple-element.200, pred[]{:T(512)S(6)} %compare.4, bf16[3,512,128]{2,1,0:T(8,128)(2,1)} %get-tuple-element.215, s32[]{:T(128)} %get-tuple-element.198, f32[512,3072]{1,0:T(8,128)} %copy-done.1, f32[512]{0:T(512)S(1)} %fusion.139, ...), kind=kOutput, calls=%fused_computation.8.clone.1 | convolution fusion | flops 411303936 | bytes 9585153 | tf_op jit(solution)/shard_map/while/body/eval_jaxpr/dot_general | solution.py:45
  184.4 3.2 multiply_reduce_fusion.2
  187.6 2.9 multiply_convert_fusion.2
  190.6 2.2 fusion.140
  192.8 1.6 fusion.141
  194.4 0.7 fusion.137
  195.1 1.1 fusion.138
  196.2 2.7 copy-done.1
  198.8 1.4 fusion.139
  200.2 6.4 %convolution_add_fusion.2 = f32[3072,128]{1,0:T(8,128)} fusion(f32[3072,128]{1,0:T(8,128)} %get-tuple-element.200, pred[]{:T(512)S(6)} %compare.4, bf16[3,512,128]{2,1,0:T(8,128)(2,1)} %get-tuple-element.215, s32[]{:T(128)} %get-tuple-element.198, f32[512,3072]{1,0:T(8,128)} %copy-done.1, f32[512]{0:T(512)S(1)} %fusion.139, ...), kind=kOutput, calls=%fused_computation.8.clone.1 | convolution fusion | flops 411303936 | bytes 9585153 | tf_op jit(solution)/shard_map/while/body/eval_jaxpr/dot_general | solution.py:45
  206.6 3.2 multiply_reduce_fusion.2
  209.8 2.9 multiply_convert_fusion.2
  212.8 3.6 fusion.140
  216.4 1.6 fusion.141
  218.7 1.1 fusion.138
  219.7 2.7 copy-done.1
  222.4 1.4 fusion.139
  223.8 6.4 %convolution_add_fusion.2 = f32[3072,128]{1,0:T(8,128)} fusion(f32[3072,128]{1,0:T(8,128)} %get-tuple-element.200, pred[]{:T(512)S(6)} %compare.4, bf16[3,512,128]{2,1,0:T(8,128)(2,1)} %get-tuple-element.215, s32[]{:T(128)} %get-tuple-element.198, f32[512,3072]{1,0:T(8,128)} %copy-done.1, f32[512]{0:T(512)S(1)} %fusion.139, ...), kind=kOutput, calls=%fused_computation.8.clone.1 | convolution fusion | flops 411303936 | bytes 9585153 | tf_op jit(solution)/shard_map/while/body/eval_jaxpr/dot_general | solution.py:45
  230.2 3.2 multiply_reduce_fusion.2
  233.4 2.9 multiply_convert_fusion.2
  236.3 3.7 fusion.140
  240.0 1.6 fusion.141
  241.7 2.1 fusion.35
  243.9 1.5 collective-permute-start
  245.4 35.8 %collective-permute-done = f32[16,96,2,1,128]{4,1,3,2,0:T(8,128)S(1)} collective-permute-done((f32[16,96,2,1,128]{4,1,3,2,0:T(8,128)S(1)}, f32[16,96,2,1,128]{4,1,3,2,0:T(8,128)S(1)}, u32[]{:S(2)}, u32[]{:S(2)}) %collective-permute-start) | collective-permute-done | bytes 1572896 | tf_op jit(solution)/shard_map/ppermute | solution.py:10
  281.5 1.1 pad_maximum_fusion
  282.6 22.8 %all_to_all.20 = bf16[16,96,3,1,128]{4,1,3,2,0:T(8,128)(2,1)S(1)} all-to-all(bf16[16,96,3,1,128]{4,1,3,2,0:T(8,128)(2,1)S(1)} %pad_maximum_fusion), channel_id=1, replica_groups=mesh['batch'=8,'seq'=16] {'seq'}, dimensions={0} | all-to-all | bytes 2359296 | tf_op jit(solution)/shard_map/all_to_all | solution.py:151
  305.5 1.8 copy.39
  307.3 3.0 reshape.115
  310.3 7.7 %fusion.79 = f32[1024,3072]{1,0:T(8,128)} fusion(bf16[192,3072]{1,0:T(8,128)(2,1)} %reshape.115, bf16[1,192,1024]{2,1,0:T(8,128)(2,1)S(1)} %copy-done.3, f32[192]{0:T(256)S(1)} %copy-done.15, f32[192]{0:T(256)S(1)} %copy-done.13), kind=kOutput, calls=%fused_computation.87 | convolution fusion | flops 1208745984 | bytes 14157312 | tf_op jit(solution)/shard_map/dot_general | solution.py:156
  318.1 5.5 %fusion.75 = (f32[192]{0:T(256)S(1)}, f32[192,1024]{1,0:T(8,128)S(1)}) fusion(bf16[1,192,1024]{2,1,0:T(8,128)(2,1)S(1)} %copy-done.3, f32[192]{0:T(256)S(1)} %copy-done.13, bf16[192,3072]{1,0:T(8,128)(2,1)} %reshape.115, bf16[1024,3072]{1,0:T(8,128)(2,1)} %param.9), kind=kOutput, calls=%fused_computation.82 | convolution fusion | flops 1208745728 | bytes 8652288 | tf_op jit(solution)/shard_map/dot_general | solution.py:162
  323.7 0.8 copy-done.8
  324.9 86.4 %reduce-scatter.3.cloned.1.call-done = f32[64,3072]{1,0:T(8,128)} async-done(((f32[1024,3072]{1,0:T(8,128)}), f32[64,3072]{1,0:T(8,128)}) %reduce-scatter.3.cloned.1.call-update) | async-done | bytes 786448 | tf_op jit(solution)/shard_map/reduce_scatter | solution.py:155
  411.3 2.2 fusion.85
  413.5 1.3 fusion.46
  414.9 60.3 %all-reduce.3.cloned.1.call-done = (f32[64,3072]{1,0:T(8,128)}, f32[64,1024]{1,0:T(8,128)}) async-done(((f32[64,3072]{1,0:T(8,128)}, f32[64,1024]{1,0:T(8,128)}), (f32[64,3072]{1,0:T(8,128)}, f32[64,1024]{1,0:T(8,128)})) %all-reduce.3.cloned.1.call-update) | async-done | bytes 1048592 | tf_op jit(solution)/shard_map/psum | solution.py:161
  475.2 2.1 copy.86
  477.3 1.7 copy.87
  (79 shorter events, 3.8 us)
Async XLA Ops:
  7.2 23.1 %copy-start = (bf16[1024,1024]{1,0:T(8,128)(2,1)S(1)}, bf16[1024,1024]{1,0:T(8,128)(2,1)}, u32[]{:S(2)}) copy-start(bf16[1024,1024]{1,0:T(8,128)(2,1)} %param.10) | copy-start | bytes 6291460
  7.2 89.0 %all-gather.5.cloned.1.call-start = ((), (), s32[]{:S(2)}) async-start(), calls=%async_computation.8 | async-start | bytes 6684672 | tf_op jit(solution)/shard_map/all_gather | solution.py:104
  8.5 6.2 %copy-start.12 = (f32[192]{0:T(256)}, f32[192]{0:T(256)S(1)}, u32[]{:S(2)}) copy-start(f32[192]{0:T(256)S(1)} %broadcast_multiply_fusion) | copy-start | bytes 2308
  9.8 0.5 copy-start.16
  10.3 4.4 copy-start.14
  16.9 141.8 %all-gather.7.cloned.1.call-start = ((), (), s32[]{:S(2)}) async-start(), calls=%async_computation.9 | async-start | bytes 6684672 | tf_op jit(solution)/shard_map/all_gather | solution.py:105
  18.9 9.8 %copy-start.4 = (bf16[192,1,8,128]{3,2,1,0:T(8,128)(2,1)S(1)}, bf16[192,1,8,128]{3,2,1,0:T(8,128)(2,1)}, u32[]{:S(2)}) copy-start(bf16[192,1,8,128]{3,2,1,0:T(8,128)(2,1)} %get-tuple-element.117) | copy-start | bytes 1179652
  18.9 11.3 %copy-start.5 = (bf16[1,192,1024]{2,1,0:T(8,128)(2,1)S(1)}, bf16[1,192,1024]{2,1,0:T(8,128)(2,1)}, u32[]{:S(2)}) copy-start(bf16[1,192,1024]{2,1,0:T(8,128)(2,1)} %param.11) | copy-start | bytes 1179652
  20.6 38.0 %all-to-all-start.1 = ((bf16[16,192,2,1,128]{4,1,3,2,0:T(8,128)(2,1)}), bf16[16,192,2,1,128]{4,1,3,2,0:T(8,128)(2,1)}, u32[]{:S(2)}, u32[]{:S(2)}) async-start(bf16[16,192,2,1,128]{4,1,3,2,0:T(8,128)(2,1)} %bitcast.192), calls=%async_computation.1 | async-start | bytes 3145728 | tf_op jit(solution)/shard_map/all_to_all | solution.py:92
  30.2 138.9 %copy-start.18 = (f32[192]{0:T(256)}, f32[192]{0:T(256)S(1)}, u32[]{:S(2)}) copy-start(f32[192]{0:T(256)S(1)} %compare_convert_fusion) | copy-start | bytes 2308
  58.7 59.9 %all-to-all-start = ((bf16[16,96,1,128]{3,1,2,0:T(8,128)(2,1)}), bf16[16,96,1,128]{3,1,2,0:T(8,128)(2,1)S(1)}, u32[]{:S(2)}, u32[]{:S(2)}) async-start(bf16[16,96,1,128]{3,1,2,0:T(8,128)(2,1)} %bitcast.11), calls=%async_computation | async-start | bytes 786432 | tf_op jit(solution)/shard_map/all_to_all | solution.py:91
  118.6 54.2 %all-to-all-start.2 = ((bf16[16,96,1,128]{3,1,2,0:T(8,128)(2,1)}), bf16[16,96,1,128]{3,1,2,0:T(8,128)(2,1)}, u32[]{:S(2)}, u32[]{:S(2)}) async-start(bf16[16,96,1,128]{3,1,2,0:T(8,128)(2,1)} %bitcast.195), calls=%async_computation.2 | async-start | bytes 786432 | tf_op jit(solution)/shard_map/all_to_all | solution.py:134
  123.1 201.8 %reduce-scatter.5.cloned.1.call-start = ((), (), s32[]{:S(2)}) async-start(), calls=%async_computation.7 | async-start | bytes 4456448 | tf_op jit(solution)/shard_map/reduce_scatter | solution.py:126
  158.7 11.3 %copy-start.6 = (bf16[1,192,1024]{2,1,0:T(8,128)(2,1)S(1)}, bf16[1,192,1024]{2,1,0:T(8,128)(2,1)}, u32[]{:S(2)}) copy-start(bf16[1,192,1024]{2,1,0:T(8,128)(2,1)} %param.11) | copy-start | bytes 1179652
  169.2 0.7 copy-start.10
  172.7 238.6 %reduce-scatter.3.cloned.1.call-start = ((), (), s32[]{:S(2)}) async-start(), calls=%async_computation.6 | async-start | bytes 13369344 | tf_op jit(solution)/shard_map/reduce_scatter | solution.py:155
  174.5 2.7 copy-start.1
  178.5 5.9 %copy-start.2 = (f32[512,3072]{1,0:T(8,128)S(1)}, f32[512,3072]{1,0:T(8,128)}, u32[]{:S(2)}) copy-start(f32[512,3072]{1,0:T(8,128)} %copy-done.1) | copy-start | bytes 18874372 | tf_op jit(solution)/shard_map/while
  178.6 5.9 %copy-start.9 = (bf16[3072,128]{1,0:T(8,128)(2,1)S(1)}, bf16[3072,128]{1,0:T(8,128)(2,1)}, u32[]{:S(2)}) copy-start(bf16[3072,128]{1,0:T(8,128)(2,1)} %get-tuple-element.216) | copy-start | bytes 2359300 | tf_op jit(solution)/shard_map/while
  196.1 2.7 copy-start.1
  200.2 6.4 %copy-start.2 = (f32[512,3072]{1,0:T(8,128)S(1)}, f32[512,3072]{1,0:T(8,128)}, u32[]{:S(2)}) copy-start(f32[512,3072]{1,0:T(8,128)} %copy-done.1) | copy-start | bytes 18874372 | tf_op jit(solution)/shard_map/while
  200.2 6.4 %copy-start.9 = (bf16[3072,128]{1,0:T(8,128)(2,1)S(1)}, bf16[3072,128]{1,0:T(8,128)(2,1)}, u32[]{:S(2)}) copy-start(bf16[3072,128]{1,0:T(8,128)(2,1)} %get-tuple-element.216) | copy-start | bytes 2359300 | tf_op jit(solution)/shard_map/while
  219.7 2.7 copy-start.1
  223.8 6.4 %copy-start.2 = (f32[512,3072]{1,0:T(8,128)S(1)}, f32[512,3072]{1,0:T(8,128)}, u32[]{:S(2)}) copy-start(f32[512,3072]{1,0:T(8,128)} %copy-done.1) | copy-start | bytes 18874372 | tf_op jit(solution)/shard_map/while
  223.8 6.4 %copy-start.9 = (bf16[3072,128]{1,0:T(8,128)(2,1)S(1)}, bf16[3072,128]{1,0:T(8,128)(2,1)}, u32[]{:S(2)}) copy-start(bf16[3072,128]{1,0:T(8,128)(2,1)} %get-tuple-element.216) | copy-start | bytes 2359300 | tf_op jit(solution)/shard_map/while
  243.9 37.4 %collective-permute-start = (f32[16,96,2,1,128]{4,1,3,2,0:T(8,128)S(1)}, f32[16,96,2,1,128]{4,1,3,2,0:T(8,128)S(1)}, u32[]{:S(2)}, u32[]{:S(2)}) collective-permute-start(f32[16,96,2,1,128]{4,1,3,2,0:T(8,128)S(1)} %bitcast.194), channel_id=1, source_target_pairs={{0,1},{1,0},{2,3},{3,2},{4,5},{5,4},{6,7},{7,6},{8,9},{9,8},{10,11... | collective-permute-start | bytes 4718600 | tf_op jit(solution)/shard_map/ppermute | solution.py:10
  281.3 29.0 %copy-start.3 = (bf16[1,192,1024]{2,1,0:T(8,128)(2,1)S(1)}, bf16[1,192,1024]{2,1,0:T(8,128)(2,1)}, u32[]{:S(2)}) copy-start(bf16[1,192,1024]{2,1,0:T(8,128)(2,1)} %param.7) | copy-start | bytes 1179652
  281.3 29.0 %copy-start.13 = (f32[192]{0:T(256)S(1)}, f32[192]{0:T(256)}, u32[]{:S(2)}) copy-start(f32[192]{0:T(256)} %copy-done.12) | copy-start | bytes 2308
  281.3 29.0 %copy-start.15 = (f32[192]{0:T(256)S(1)}, f32[192]{0:T(256)}, u32[]{:S(2)}) copy-start(f32[192]{0:T(256)} %copy-done.14) | copy-start | bytes 2308
  318.0 5.6 %copy-start.17 = (f32[192]{0:T(256)S(1)}, f32[192]{0:T(256)}, u32[]{:S(2)}) copy-start(f32[192]{0:T(256)} %copy-done.16) | copy-start | bytes 2308
  318.1 93.3 %copy-start.7 = (bf16[1,192,1024]{2,1,0:T(8,128)(2,1)S(1)}, bf16[1,192,1024]{2,1,0:T(8,128)(2,1)}, u32[]{:S(2)}) copy-start(bf16[1,192,1024]{2,1,0:T(8,128)(2,1)} %param.11) | copy-start | bytes 1179652
  318.1 95.5 %copy-start.11 = (bf16[8,24,8,128]{3,2,1,0:T(8,128)(2,1)S(1)}, bf16[8,24,8,128]{3,2,1,0:T(8,128)(2,1)}, u32[]{:S(2)}) copy-start(bf16[8,24,8,128]{3,2,1,0:T(8,128)(2,1)} %copy-done.10) | copy-start | bytes 1179652
  318.1 95.5 %copy-start.19 = (f32[192]{0:T(256)S(1)}, f32[192]{0:T(256)}, u32[]{:S(2)}) copy-start(f32[192]{0:T(256)} %copy-done.18) | copy-start | bytes 2308
  318.1 157.1 %all-reduce.3.cloned.1.call-start = ((), (), s32[]{:S(2)}) async-start(), calls=%async_computation.10 | async-start | bytes 2097152 | tf_op jit(solution)/shard_map/psum | solution.py:161
  323.7 0.9 copy-start.8
Sparse Core Ops, SparseCore 0:
  17.0 79.0 all-gather.4
  98.3 60.3 all-gather.6
  172.8 77.9 reduce-scatter.4
  318.2 93.0 reduce-scatter.2
  413.6 61.5 all-reduce.2
where the time goes:
time: 487 us; the launch traced here: 485 us
  waiting for transfers between devices  276 us (57%)
  matrix products  91.2 us (19%)
  other arithmetic  33.6 us (7%)
  local copies, waits for them, and re-layouts  28.7 us (6%)
  blocking collectives  22.8 us (5%)
  starting transfers between devices  18 us (4%)
  between operations  14.8 us (3%)
    reduce_scatter x1, waiting for transfers between devices, per_device(): lax.psum_scatter(jnp.dot(columns.T, dqkv, preferred_element_type=jnp.floa...  86.4 us
    psum x1, waiting for transfers between devices, per_device(): grad_qkv, grad_out = lax.psum((qkv_share, out_share), 'batch')  60.3 us
    ppermute x1, waiting for transfers between devices, from_partner(): lax.ppermute(array, axis, [(i, i ^ 1 << stride) for i in range(lax.axis_s...  35.8 us
    all_gather x1, waiting for transfers between devices, per_device(): value_piece = lax.all_gather(qkv_local[:, 2], 'seq', axis=0, tiled=True)  35.3 us
    all_gather x1, waiting for transfers between devices, per_device(): key_piece = lax.all_gather(qkv_local[:, 1], 'seq', axis=0, tiled=True)  31.5 us
    all_to_all x1, waiting for transfers between devices, per_device(): lax.all_to_all(paired_send, 'seq', split_axis=0, concat_axis=0, tiled=True)  26.6 us
    all_to_all x1, blocking collectives, per_device(): lax.all_to_all(dtrio, 'seq', split_axis=0, concat_axis=0, tiled=True)  22.8 us
    dot_general x3, matrix products, step(): jnp.dot(p_half.T, d_rows, preferred_element_type=jnp.float32)  18.6 us
  transfers between devices with their start and end apart: 9, of which 6 were waited for; matrix products, arithmetic and copies ran while one was open for 27% of the time, Pallas kernels for 0%

commit v1 on v0

--- a/solution.py
+++ b/solution.py
@@ -101,7 +101,9 @@
     valid = (own_pos < length).astype(jnp.float32)
     query = qkv_local[:, 0]
     top = jnp.full((H, tok_rows), -1e30, jnp.float32)
-    key_piece = lax.all_gather(qkv_local[:, 1], "seq", axis=0, tiled=True)
+    key_piece = jnp.concatenate(
+        lax.all_to_all(jnp.stack([qkv_local[:, 1]] * lax.axis_size("seq")), "seq", 0, 0), axis=0
+    )
     value_piece = lax.all_gather(qkv_local[:, 2], "seq", axis=0, tiled=True)
     key_pos = jnp.arange(key_piece.shape[0], dtype=jnp.int32)
     key_bias = jnp.where(key_pos < length, 0.0, -1000000000.0).astype(jnp.float32)

time: 487 us -> 539 us (1.11)
  waiting for transfers between devices: 276 us -> 315 us
  starting transfers between devices: 18 us -> 30.2 us
  local copies, waits for them, and re-layouts: 28.7 us -> 34.7 us
    all_to_all x0 -> x1, waiting for transfers between devices: none -> 102 us  [per_device(): lax.all_to_all(jnp.stack([qkv_local[:, 1]] * lax.axis_size('seq')), 'seq'...]
    all_gather x1, waiting for transfers between devices: 35.3 us -> 0.02 us  [per_device(): value_piece = lax.all_gather(qkv_local[:, 2], 'seq', axis=0, tiled=True)]
    all_gather x1 -> x0, waiting for transfers between devices: 31.5 us -> none  [per_device(): key_piece = lax.all_gather(qkv_local[:, 1], 'seq', axis=0, tiled=True)]
  transfers between devices with their start and end apart: 9 -> 9, of which waited for: 6 -> 5; matrix products, arithmetic and copies ran while one was open for 27% -> 25% of each run, Pallas kernels for 0% -> 0%
where the time goes in v1:
time: 539 us; the launch traced here: 538 us
  waiting for transfers between devices  315 us (58%)
  matrix products  87 us (16%)
  local copies, waits for them, and re-layouts  34.7 us (6%)
  other arithmetic  33.4 us (6%)
  starting transfers between devices  30.2 us (6%)
  blocking collectives  22.8 us (4%)
  between operations  14.8 us (3%)
    all_to_all x1, waiting for transfers between devices, per_device(): lax.all_to_all(jnp.stack([qkv_local[:, 1]] * lax.axis_size('seq')), 'seq'...  102 us
    reduce_scatter x1, waiting for transfers between devices, per_device(): lax.psum_scatter(jnp.dot(columns.T, dqkv, preferred_element_type=jnp.floa...  87.8 us
    psum x1, waiting for transfers between devices, per_device(): grad_qkv, grad_out = lax.psum((qkv_share, out_share), 'batch')  60.3 us
    ppermute x1, waiting for transfers between devices, from_partner(): lax.ppermute(array, axis, [(i, i ^ 1 << stride) for i in range(lax.axis_s...  34.8 us
    all_to_all x1, waiting for transfers between devices, per_device(): lax.all_to_all(paired_send, 'seq', split_axis=0, concat_axis=0, tiled=True)  29.6 us
    all_to_all x1, blocking collectives, per_device(): lax.all_to_all(dtrio, 'seq', split_axis=0, concat_axis=0, tiled=True)  22.8 us
    dot_general x3, matrix products, step(): jnp.dot(p_half.T, d_rows, preferred_element_type=jnp.float32)  18.6 us
  transfers between devices with their start and end apart: 9, of which 5 were waited for; matrix products, arithmetic and copies ran while one was open for 25% of the time, Pallas kernels for 0%

profile of v1, /device:TPU:0, one launch (start us, length us, event | category | flops | bytes accessed | tf_op | source)
XLA Modules:
  0.0 537.8 jit_solution(10099832365569063754)
XLA Ops:
  7.2 1.3 convert_reduce_fusion
  8.5 1.2 fusion.71
  10.3 4.4 fusion.36
  15.0 1.1 fusion.103
  16.1 0.8 copy.43
  17.3 1.5 broadcast_in_dim.61
  18.8 8.0 %all-to-all-start.2 = ((bf16[16,192,2,1,128]{4,1,3,2,0:T(8,128)(2,1)}), bf16[16,192,2,1,128]{4,1,3,2,0:T(8,128)(2,1)}, u32[]{:S(2)}, u32[]{:S(2)}) async-start(bf16[16,192,2,1,128]{4,1,3,2,0:T(8,128)(2,1)} %bitcast.192), calls=%async_computation.2 | async-start | bytes 3145728 | tf_op jit(solution)/shard_map/all_to_all | solution.py:92
  26.9 29.6 %all-to-all-done.2 = bf16[16,192,2,1,128]{4,1,3,2,0:T(8,128)(2,1)} async-done(((bf16[16,192,2,1,128]{4,1,3,2,0:T(8,128)(2,1)}), bf16[16,192,2,1,128]{4,1,3,2,0:T(8,128)(2,1)}, u32[]{:S(2)}, u32[]{:S(2)}) %all-to-all-start.2) | async-done | bytes 1572896 | tf_op jit(solution)/shard_map/all_to_all | solution.py:92
  56.5 4.3 stack.12
  60.7 4.8 all-to-all-start
  65.6 0.8 copy.42
  67.1 0.9 fusion.45
  68.0 0.8 copy.36
  68.9 2.4 fusion.102
  71.2 102.1 %all-to-all-done = bf16[16,192,8,128]{3,1,2,0:T(8,128)(2,1)} async-done(((bf16[16,192,8,128]{3,1,2,0:T(8,128)(2,1)}), bf16[16,192,8,128]{3,1,2,0:T(8,128)(2,1)}, u32[]{:S(2)}, u32[]{:S(2)}) %all-to-all-start) | async-done | bytes 6291488 | tf_op jit(solution)/shard_map/all_to_all | solution.py:105
  173.3 7.5 %all-to-all-start.1 = ((bf16[16,96,1,128]{3,1,2,0:T(8,128)(2,1)}), bf16[16,96,1,128]{3,1,2,0:T(8,128)(2,1)S(1)}, u32[]{:S(2)}, u32[]{:S(2)}) async-start(bf16[16,96,1,128]{3,1,2,0:T(8,128)(2,1)} %bitcast.196), calls=%async_computation.1 | async-start | bytes 786432 | tf_op jit(solution)/shard_map/all_to_all | solution.py:91
  180.8 3.4 copy.32
  184.3 7.9 %fusion.26 = (f32[8,192]{1,0:T(8,128)S(1)}, f32[8,192,3072]{2,1,0:T(8,128)}) fusion(f32[3072]{0:T(1024)S(1)} %fusion.97, bf16[3072,8,128]{2,0,1:T(8,128)(2,1)S(1)} %bitcast.187, bf16[192,1,8,128]{3,2,1,0:T(8,128)(2,1)S(1)} %copy-done.5), kind=kOutput, calls=%fused_computation.34 | convolution fusion | flops 1222113792 | bytes 25577472 | tf_op jit(solution)/shard_map/qhd,khd->hqk/dot_general | solution.py:111
  192.2 10.2 %fusion.27 = f32[8,192]{1,0:T(8,128)S(1)} fusion(f32[8,192,3072]{2,1,0:T(8,128)} %get-tuple-element.121, f32[8,192]{1,0:T(8,128)S(1)} %broadcast_maximum_fusion, f32[3072]{0:T(1024)S(1)} %fusion.97), kind=kLoop, calls=%fused_computation.35 | loop fusion | flops 18872832 | bytes 18898944 | tf_op jit(solution)/shard_map/reduce_sum | solution.py:116
  202.3 7.3 %all-to-all-start.3 = ((bf16[16,96,1,128]{3,1,2,0:T(8,128)(2,1)}), bf16[16,96,1,128]{3,1,2,0:T(8,128)(2,1)}, u32[]{:S(2)}, u32[]{:S(2)}) async-start(bf16[16,96,1,128]{3,1,2,0:T(8,128)(2,1)} %bitcast.195), calls=%async_computation.3 | async-start | bytes 786432 | tf_op jit(solution)/shard_map/all_to_all | solution.py:136
  209.9 10.5 %fusion.63 = bf16[8,24,8,128]{3,2,1,0:T(8,128)(2,1)S(1)} fusion(bf16[3072,1,8,128]{3,0,2,1:T(8,128)(2,1)} %all-gather.3.cloned.1.call-done, f32[8,192,3072]{2,1,0:T(8,128)} %get-tuple-element.121, f32[8,192]{1,0:T(8,128)S(1)} %broadcast_maximum_fusion, f32[3072]{0:T(1024)S(1)} %fusion.97, f32[192,8]{0,1:T(8,128)S(1)} %bitcast.200), kind=kOutput, calls=%fused_computation.74 | convolution fusion | flops 1227227136 | bytes 25583616 | tf_op jit(solution)/shard_map/hqk,khd->hqd/dot_general | solution.py:117
  220.4 0.7 copy-done.12
  221.2 2.7 fusion.81
  224.0 69.0 %while.15 = (s32[]{:T(128)}, f32[3072,128]{1,0:T(8,128)}, f32[3072,128]{1,0:T(8,128)}, bf16[3,512,128]{2,1,0:T(8,128)(2,1)}, bf16[3,512,128]{2,1,0:T(8,128)(2,1)...) while((s32[]{:T(128)}, f32[3072,128]{1,0:T(8,128)}, ...), condition=%wide.region_8.9_spmd.clone, body=%wide.region_4.0_spmd.clone.sunk | while | flops 2054689280 | bytes 116358872 | solution.py:49
  224.7 1.1 fusion.138
  225.7 2.7 copy-done.1
  228.4 1.4 fusion.139
  229.8 5.9 %convolution_add_fusion.2 = f32[3072,128]{1,0:T(8,128)} fusion(f32[3072,128]{1,0:T(8,128)} %get-tuple-element.200, pred[]{:T(512)S(6)} %compare.4, bf16[3,512,128]{2,1,0:T(8,128)(2,1)} %get-tuple-element.215, s32[]{:T(128)} %get-tuple-element.198, f32[512,3072]{1,0:T(8,128)} %copy-done.1, f32[512]{0:T(512)S(1)} %fusion.139, ...), kind=kOutput, calls=%fused_computation.8.clone.1 | convolution fusion | flops 411303936 | bytes 9585153 | tf_op jit(solution)/shard_map/while/body/eval_jaxpr/dot_general | solution.py:45
  235.6 3.2 multiply_reduce_fusion.2
  238.9 2.9 multiply_convert_fusion.2
  241.8 2.3 fusion.140
  244.1 1.6 fusion.141
  246.4 1.1 fusion.138
  247.4 2.7 copy-done.1
  250.1 1.4 fusion.139
  251.5 6.3 %convolution_add_fusion.2 = f32[3072,128]{1,0:T(8,128)} fusion(f32[3072,128]{1,0:T(8,128)} %get-tuple-element.200, pred[]{:T(512)S(6)} %compare.4, bf16[3,512,128]{2,1,0:T(8,128)(2,1)} %get-tuple-element.215, s32[]{:T(128)} %get-tuple-element.198, f32[512,3072]{1,0:T(8,128)} %copy-done.1, f32[512]{0:T(512)S(1)} %fusion.139, ...), kind=kOutput, calls=%fused_computation.8.clone.1 | convolution fusion | flops 411303936 | bytes 9585153 | tf_op jit(solution)/shard_map/while/body/eval_jaxpr/dot_general | solution.py:45
  257.8 3.2 multiply_reduce_fusion.2
  261.1 2.9 multiply_convert_fusion.2
  264.0 3.7 fusion.140
  267.7 1.6 fusion.141
  270.0 1.1 fusion.138
  271.0 2.7 copy-done.1
  273.7 1.4 fusion.139
  275.1 6.4 %convolution_add_fusion.2 = f32[3072,128]{1,0:T(8,128)} fusion(f32[3072,128]{1,0:T(8,128)} %get-tuple-element.200, pred[]{:T(512)S(6)} %compare.4, bf16[3,512,128]{2,1,0:T(8,128)(2,1)} %get-tuple-element.215, s32[]{:T(128)} %get-tuple-element.198, f32[512,3072]{1,0:T(8,128)} %copy-done.1, f32[512]{0:T(512)S(1)} %fusion.139, ...), kind=kOutput, calls=%fused_computation.8.clone.1 | convolution fusion | flops 411303936 | bytes 9585153 | tf_op jit(solution)/shard_map/while/body/eval_jaxpr/dot_general | solution.py:45
  281.5 3.2 multiply_reduce_fusion.2
  284.7 2.9 multiply_convert_fusion.2
  287.6 3.7 fusion.140
  291.3 1.6 fusion.141
  293.0 2.1 fusion.33
  295.1 2.3 collective-permute-start
  297.4 34.8 %collective-permute-done = f32[16,96,2,1,128]{4,1,3,2,0:T(8,128)S(1)} collective-permute-done((f32[16,96,2,1,128]{4,1,3,2,0:T(8,128)S(1)}, f32[16,96,2,1,128]{4,1,3,2,0:T(8,128)S(1)}, u32[]{:S(2)}, u32[]{:S(2)}) %collective-permute-start) | collective-permute-done | bytes 1572896 | tf_op jit(solution)/shard_map/ppermute | solution.py:10
  332.5 1.1 pad_maximum_fusion
  333.6 22.8 %all_to_all.25 = bf16[16,96,3,1,128]{4,1,3,2,0:T(8,128)(2,1)S(1)} all-to-all(bf16[16,96,3,1,128]{4,1,3,2,0:T(8,128)(2,1)S(1)} %pad_maximum_fusion), channel_id=1, replica_groups=mesh['batch'=8,'seq'=16] {'seq'}, dimensions={0} | all-to-all | bytes 2359296 | tf_op jit(solution)/shard_map/all_to_all | solution.py:153
  356.4 1.8 copy.40
  358.2 3.0 reshape.121
  361.2 7.7 %fusion.77 = f32[1024,3072]{1,0:T(8,128)} fusion(bf16[192,3072]{1,0:T(8,128)(2,1)} %reshape.121, bf16[1,192,1024]{2,1,0:T(8,128)(2,1)S(1)} %copy-done.3, f32[192]{0:T(256)S(1)} %copy-done.17, f32[192]{0:T(256)S(1)} %copy-done.15), kind=kOutput, calls=%fused_computation.85 | convolution fusion | flops 1208745984 | bytes 14157312 | tf_op jit(solution)/shard_map/dot_general | solution.py:158
  369.1 5.5 %fusion.73 = (f32[192]{0:T(256)S(1)}, f32[192,1024]{1,0:T(8,128)S(1)}) fusion(bf16[1,192,1024]{2,1,0:T(8,128)(2,1)S(1)} %copy-done.3, f32[192]{0:T(256)S(1)} %copy-done.15, bf16[192,3072]{1,0:T(8,128)(2,1)} %reshape.121, bf16[1024,3072]{1,0:T(8,128)(2,1)} %param.9), kind=kOutput, calls=%fused_computation.80 | convolution fusion | flops 1208745728 | bytes 8652288 | tf_op jit(solution)/shard_map/dot_general | solution.py:164
  374.6 0.8 copy-done.9
  375.8 87.8 %reduce-scatter.3.cloned.1.call-done = f32[64,3072]{1,0:T(8,128)} async-done(((f32[1024,3072]{1,0:T(8,128)}), f32[64,3072]{1,0:T(8,128)}) %reduce-scatter.3.cloned.1.call-update) | async-done | bytes 786448 | tf_op jit(solution)/shard_map/reduce_scatter | solution.py:157
  463.7 2.2 fusion.83
  465.9 1.3 fusion.44
  467.2 60.3 %all-reduce.3.cloned.1.call-done = (f32[64,3072]{1,0:T(8,128)}, f32[64,1024]{1,0:T(8,128)}) async-done(((f32[64,3072]{1,0:T(8,128)}, f32[64,1024]{1,0:T(8,128)}), (f32[64,3072]{1,0:T(8,128)}, f32[64,1024]{1,0:T(8,128)})) %all-reduce.3.cloned.1.call-update) | async-done | bytes 1048592 | tf_op jit(solution)/shard_map/psum | solution.py:163
  527.6 2.1 copy.86
  529.6 1.7 copy.87
  (84 shorter events, 4.5 us)
Async XLA Ops:
  7.2 59.9 %copy-start = (bf16[1024,1024]{1,0:T(8,128)(2,1)S(1)}, bf16[1024,1024]{1,0:T(8,128)(2,1)}, u32[]{:S(2)}) copy-start(bf16[1024,1024]{1,0:T(8,128)(2,1)} %param.10) | copy-start | bytes 6291460
  7.2 202.7 %all-gather.3.cloned.1.call-start = ((), (), s32[]{:S(2)}) async-start(), calls=%async_computation.9 | async-start | bytes 6684672 | tf_op jit(solution)/shard_map/all_gather | solution.py:107
  8.5 6.3 %copy-start.14 = (f32[192]{0:T(256)}, f32[192]{0:T(256)S(1)}, u32[]{:S(2)}) copy-start(f32[192]{0:T(256)S(1)} %broadcast_multiply_fusion) | copy-start | bytes 2308
  9.8 0.6 copy-start.18
  10.3 4.4 copy-start.16
  17.1 9.8 %copy-start.10 = (bf16[192,8,128]{2,1,0:T(8,128)(2,1)S(1)}, bf16[192,8,128]{2,1,0:T(8,128)(2,1)}, u32[]{:S(2)}) copy-start(bf16[192,8,128]{2,1,0:T(8,128)(2,1)} %get-tuple-element.118) | copy-start | bytes 1179652
  18.8 37.7 %all-to-all-start.2 = ((bf16[16,192,2,1,128]{4,1,3,2,0:T(8,128)(2,1)}), bf16[16,192,2,1,128]{4,1,3,2,0:T(8,128)(2,1)}, u32[]{:S(2)}, u32[]{:S(2)}) async-start(bf16[16,192,2,1,128]{4,1,3,2,0:T(8,128)(2,1)} %bitcast.192), calls=%async_computation.2 | async-start | bytes 3145728 | tf_op jit(solution)/shard_map/all_to_all | solution.py:92
  60.7 4.8 copy-start.4
  60.7 6.3 %copy-start.6 = (bf16[1,192,1024]{2,1,0:T(8,128)(2,1)S(1)}, bf16[1,192,1024]{2,1,0:T(8,128)(2,1)}, u32[]{:S(2)}) copy-start(bf16[1,192,1024]{2,1,0:T(8,128)(2,1)} %param.11) | copy-start | bytes 1179652
  60.7 112.6 %all-to-all-start = ((bf16[16,192,8,128]{3,1,2,0:T(8,128)(2,1)}), bf16[16,192,8,128]{3,1,2,0:T(8,128)(2,1)}, u32[]{:S(2)}, u32[]{:S(2)}) async-start(bf16[16,192,8,128]{3,1,2,0:T(8,128)(2,1)} %stack.12), calls=%async_computation | async-start | bytes 12582912 | tf_op jit(solution)/shard_map/all_to_all | solution.py:105
  67.1 153.3 %copy-start.20 = (f32[192]{0:T(256)}, f32[192]{0:T(256)S(1)}, u32[]{:S(2)}) copy-start(f32[192]{0:T(256)S(1)} %compare_convert_fusion) | copy-start | bytes 2308
  173.3 29.0 %all-to-all-start.1 = ((bf16[16,96,1,128]{3,1,2,0:T(8,128)(2,1)}), bf16[16,96,1,128]{3,1,2,0:T(8,128)(2,1)S(1)}, u32[]{:S(2)}, u32[]{:S(2)}) async-start(bf16[16,96,1,128]{3,1,2,0:T(8,128)(2,1)} %bitcast.196), calls=%async_computation.1 | async-start | bytes 786432 | tf_op jit(solution)/shard_map/all_to_all | solution.py:91
  180.8 3.4 copy-start.5
  202.3 21.6 %all-to-all-start.3 = ((bf16[16,96,1,128]{3,1,2,0:T(8,128)(2,1)}), bf16[16,96,1,128]{3,1,2,0:T(8,128)(2,1)}, u32[]{:S(2)}, u32[]{:S(2)}) async-start(bf16[16,96,1,128]{3,1,2,0:T(8,128)(2,1)} %bitcast.195), calls=%async_computation.3 | async-start | bytes 786432 | tf_op jit(solution)/shard_map/all_to_all | solution.py:136
  209.6 166.2 %reduce-scatter.5.cloned.1.call-start = ((), (), s32[]{:S(2)}) async-start(), calls=%async_computation.8 | async-start | bytes 4456448 | tf_op jit(solution)/shard_map/reduce_scatter | solution.py:128
  209.9 11.3 %copy-start.7 = (bf16[1,192,1024]{2,1,0:T(8,128)(2,1)S(1)}, bf16[1,192,1024]{2,1,0:T(8,128)(2,1)}, u32[]{:S(2)}) copy-start(bf16[1,192,1024]{2,1,0:T(8,128)(2,1)} %param.11) | copy-start | bytes 1179652
  220.4 0.7 copy-start.12
  223.9 239.7 %reduce-scatter.3.cloned.1.call-start = ((), (), s32[]{:S(2)}) async-start(), calls=%async_computation.7 | async-start | bytes 13369344 | tf_op jit(solution)/shard_map/reduce_scatter | solution.py:157
  225.7 2.7 copy-start.1
  229.8 5.9 %copy-start.2 = (f32[512,3072]{1,0:T(8,128)S(1)}, f32[512,3072]{1,0:T(8,128)}, u32[]{:S(2)}) copy-start(f32[512,3072]{1,0:T(8,128)} %copy-done.1) | copy-start | bytes 18874372 | tf_op jit(solution)/shard_map/while
  229.8 5.9 %copy-start.11 = (bf16[3072,128]{1,0:T(8,128)(2,1)S(1)}, bf16[3072,128]{1,0:T(8,128)(2,1)}, u32[]{:S(2)}) copy-start(bf16[3072,128]{1,0:T(8,128)(2,1)} %get-tuple-element.216) | copy-start | bytes 2359300 | tf_op jit(solution)/shard_map/while
  247.4 2.7 copy-start.1
  251.5 6.4 %copy-start.2 = (f32[512,3072]{1,0:T(8,128)S(1)}, f32[512,3072]{1,0:T(8,128)}, u32[]{:S(2)}) copy-start(f32[512,3072]{1,0:T(8,128)} %copy-done.1) | copy-start | bytes 18874372 | tf_op jit(solution)/shard_map/while
  251.5 6.3 %copy-start.11 = (bf16[3072,128]{1,0:T(8,128)(2,1)S(1)}, bf16[3072,128]{1,0:T(8,128)(2,1)}, u32[]{:S(2)}) copy-start(bf16[3072,128]{1,0:T(8,128)(2,1)} %get-tuple-element.216) | copy-start | bytes 2359300 | tf_op jit(solution)/shard_map/while
  271.0 2.7 copy-start.1
  275.1 6.4 %copy-start.2 = (f32[512,3072]{1,0:T(8,128)S(1)}, f32[512,3072]{1,0:T(8,128)}, u32[]{:S(2)}) copy-start(f32[512,3072]{1,0:T(8,128)} %copy-done.1) | copy-start | bytes 18874372 | tf_op jit(solution)/shard_map/while
  275.1 6.4 %copy-start.11 = (bf16[3072,128]{1,0:T(8,128)(2,1)S(1)}, bf16[3072,128]{1,0:T(8,128)(2,1)}, u32[]{:S(2)}) copy-start(bf16[3072,128]{1,0:T(8,128)(2,1)} %get-tuple-element.216) | copy-start | bytes 2359300 | tf_op jit(solution)/shard_map/while
  295.1 37.1 %collective-permute-start = (f32[16,96,2,1,128]{4,1,3,2,0:T(8,128)S(1)}, f32[16,96,2,1,128]{4,1,3,2,0:T(8,128)S(1)}, u32[]{:S(2)}, u32[]{:S(2)}) collective-permute-start(f32[16,96,2,1,128]{4,1,3,2,0:T(8,128)S(1)} %bitcast.194), channel_id=1, source_target_pairs={{0,1},{1,0},{2,3},{3,2},{4,5},{5,4},{6,7},{7,6},{8,9},{9,8},{10,11... | collective-permute-start | bytes 4718600 | tf_op jit(solution)/shard_map/ppermute | solution.py:10
  332.2 29.0 %copy-start.3 = (bf16[1,192,1024]{2,1,0:T(8,128)(2,1)S(1)}, bf16[1,192,1024]{2,1,0:T(8,128)(2,1)}, u32[]{:S(2)}) copy-start(bf16[1,192,1024]{2,1,0:T(8,128)(2,1)} %param.7) | copy-start | bytes 1179652
  332.2 29.0 %copy-start.15 = (f32[192]{0:T(256)S(1)}, f32[192]{0:T(256)}, u32[]{:S(2)}) copy-start(f32[192]{0:T(256)} %copy-done.14) | copy-start | bytes 2308
  332.2 29.0 %copy-start.17 = (f32[192]{0:T(256)S(1)}, f32[192]{0:T(256)}, u32[]{:S(2)}) copy-start(f32[192]{0:T(256)} %copy-done.16) | copy-start | bytes 2308
  369.0 5.6 %copy-start.19 = (f32[192]{0:T(256)S(1)}, f32[192]{0:T(256)}, u32[]{:S(2)}) copy-start(f32[192]{0:T(256)} %copy-done.18) | copy-start | bytes 2308
  369.0 94.7 %copy-start.8 = (bf16[1,192,1024]{2,1,0:T(8,128)(2,1)S(1)}, bf16[1,192,1024]{2,1,0:T(8,128)(2,1)}, u32[]{:S(2)}) copy-start(bf16[1,192,1024]{2,1,0:T(8,128)(2,1)} %param.11) | copy-start | bytes 1179652
  369.0 96.9 %copy-start.13 = (bf16[8,24,8,128]{3,2,1,0:T(8,128)(2,1)S(1)}, bf16[8,24,8,128]{3,2,1,0:T(8,128)(2,1)}, u32[]{:S(2)}) copy-start(bf16[8,24,8,128]{3,2,1,0:T(8,128)(2,1)} %copy-done.12) | copy-start | bytes 1179652
  369.0 96.9 %copy-start.21 = (f32[192]{0:T(256)S(1)}, f32[192]{0:T(256)}, u32[]{:S(2)}) copy-start(f32[192]{0:T(256)} %copy-done.20) | copy-start | bytes 2308
  369.0 158.5 %all-reduce.3.cloned.1.call-start = ((), (), s32[]{:S(2)}) async-start(), calls=%async_computation.10 | async-start | bytes 2097152 | tf_op jit(solution)/shard_map/psum | solution.py:163
  374.6 0.9 copy-start.9
Sparse Core Ops, SparseCore 0:
  17.0 139.6 all-gather.2
  224.0 82.9 reduce-scatter.4
  369.1 94.5 reduce-scatter.2
  465.9 61.5 all-reduce.2
